TPU v7x, 256 devices: a whole 4x4x8 slice. The times are simulated.
256 devices in a mesh: wide: 64 (over y, z, core), seq: 4 (over x).
Axes of the slice: x: 4, y: 4, z: 8, core: 2. Of those that a mesh axis runs over, the one named last changes fastest.
Arguments:
- power: bfloat16 [160, 2097152], P('seq', 'wide')
- bin_index: int32 [160], P('seq'), may hold values from 0 to 7, as said below
- session: int32 [16384], replicated, may hold values from 0 to 63, as said below
- readin_weight: bfloat16 [64, 128, 2048], P('wide'), may hold values from -0.5 to 0.5
- qkv_weight: bfloat16 [2048, 1536], replicated, may hold values from -0.125 to 0.125
Outputs:
- heads: bfloat16 [16384, 8, 1024], P(('wide', 'seq'))
Inputs may be any that keep to these rules, and one draw needn't show every extreme that they name: `bin_index`: the samples j * 40 to (j + 1) * 40 - 1 name only bins j * 2 to (j + 1) * 2 - 1. In each aligned block of 64 patches (patches k * 64 to (k + 1) * 64 - 1) no session is named by more than 2 patches; one session, the same for every block, is named by exactly 2 patches of every block.
All inputs are finite; a program needn't handle non-finite values.
Results may differ from a plain program's by a relative error of at most 0.008.
Values may be sent and summed in bfloat16 or wider, within the bound.
No kernel may reach another device: no remote copies, remote signals or barrier semaphores. Data moves between devices by JAX's collectives and lax.ppermute only.
A program may use at most 64 MiB of HBM per device.

v0:
```python
import jax
import jax.numpy as jnp
from jax import lax
from jax.sharding import PartitionSpec as P

CH = 128
HD = 128
HEADS = 8
KVH = 2
SPB = 20


def attention_heads(qkv_rows):
    row_count = qkv_rows.shape[0]
    length = qkv_rows.shape[1]
    group_size = HEADS // KVH
    values = qkv_rows.astype(jnp.float32)
    queries = values[:, :, : HEADS * HD].reshape(row_count, length, KVH, group_size, HD)
    key_rows = values[:, :, HEADS * HD : (HEADS + KVH) * HD].reshape(row_count, length, KVH, HD)
    value_rows = values[:, :, (HEADS + KVH) * HD :].reshape(row_count, length, KVH, HD)
    queries = queries / jnp.sqrt(jnp.mean(queries * queries, axis=-1, keepdims=True) + 1e-06)
    key_rows = key_rows / jnp.sqrt(jnp.mean(key_rows * key_rows, axis=-1, keepdims=True) + 1e-06)
    scores = jnp.einsum("pigrd,pjgd->pgrij", queries, key_rows) / HD**0.5
    exponent = jnp.exp(scores)
    weights = (exponent / jnp.sum(exponent, axis=-1, keepdims=True)).astype(jnp.bfloat16)
    mixed = jnp.einsum("pgrij,pjgd->pigrd", weights.astype(jnp.float32), value_rows)
    return mixed.reshape(row_count, length, HEADS * HD).astype(jnp.bfloat16)


def project_rows(tokens, qkv_weight):
    product = jnp.dot(
        tokens.reshape(-1, tokens.shape[-1]), qkv_weight, preferred_element_type=jnp.float32
    )
    return product.astype(jnp.bfloat16).reshape(tokens.shape[:-1] + (qkv_weight.shape[1],))


def readin_rows(slab, weight_block):
    tokens = jnp.einsum(
        "abtc,cd->abtd", slab, weight_block, preferred_element_type=jnp.float32
    ).astype(jnp.bfloat16)
    return tokens


def slot_ranks(owner_ids, wide_count):
    owner_marks = (owner_ids[..., None] == jnp.arange(wide_count, dtype=jnp.int32)).astype(
        jnp.int32
    )
    running = jnp.cumsum(owner_marks, axis=-2)
    return jnp.sum(owner_marks * running, axis=-1) - 1


def body(power, bin_index, session, readin_weight, qkv_weight):
    wide_count = lax.axis_size("wide")
    seq_count = lax.axis_size("seq")
    wide_index = lax.axis_index("wide")
    seq_index = lax.axis_index("seq")
    sample_rows, channels = power.shape
    patch_count = channels // CH
    quarter = patch_count // seq_count
    bin_count = sample_rows // SPB
    capacity = max(2, 2 * quarter // wide_count)
    signal = power.astype(jnp.float32)
    squares = lax.psum(jnp.sum(signal * signal, axis=0), "seq")
    inv_rms = 1.0 / jnp.sqrt(squares / (sample_rows * seq_count) + 1e-06)
    active = jnp.maximum(signal * inv_rms[None, :] - 0.8, 0.0)
    local_bins = bin_index - seq_index * bin_count
    onehot = (local_bins[:, None] == jnp.arange(bin_count, dtype=jnp.int32)[None, :]).astype(
        jnp.float32
    )
    binned = (jnp.dot(onehot.T, active, precision=lax.Precision.HIGHEST) * (1.0 / SPB)).astype(
        jnp.bfloat16
    )
    patches = binned.reshape(bin_count, patch_count, CH).transpose(1, 0, 2)
    owners = lax.dynamic_slice_in_dim(session, wide_index * patch_count, patch_count)
    weight_block = readin_weight[0]
    owner_grid = owners.reshape(seq_count, quarter)
    slot_rank = slot_ranks(owner_grid, wide_count)
    quarter_ids = jnp.arange(seq_count, dtype=jnp.int32)[:, None]
    slot_index = ((owner_grid * seq_count + quarter_ids) * capacity + slot_rank).reshape(
        patch_count
    )
    slot_count = seq_count * capacity
    length = patches.shape[1]
    outgoing = (
        jnp.zeros((wide_count * slot_count, length, CH), jnp.bfloat16).at[slot_index].set(patches)
    )
    outgoing = outgoing.reshape(wide_count, slot_count, length, CH)
    returned_rows = lax.all_to_all(
        readin_rows(
            lax.all_to_all(outgoing, "wide", split_axis=0, concat_axis=0, tiled=True), weight_block
        ),
        "wide",
        split_axis=0,
        concat_axis=0,
        tiled=True,
    )
    arrived = returned_rows.reshape(
        wide_count * slot_count, returned_rows.shape[2], returned_rows.shape[3]
    )[slot_index]
    arrived = lax.all_to_all(arrived, "seq", split_axis=0, concat_axis=1, tiled=True)
    projected = project_rows(arrived, qkv_weight)
    return attention_heads(projected)


def solution(mesh):
    placed = (P("seq", "wide"), P("seq"), P(), P("wide", None, None), P())
    return jax.shard_map(
        body, mesh=mesh, in_specs=placed, out_specs=P(("wide", "seq"), None, None), check_vma=False
    )
```

profile of v0, /device:TPU:1, one launch (start us, length us, event | category | flops | bytes accessed | tf_op | source)
XLA Modules:
  0.0 287.6 jit_solution(8272917020949830205)
XLA Ops:
  6.5 0.0 copy-start
  6.5 0.0 copy-start.1
  6.5 0.0 copy-start.3
  6.5 0.0 all-reduce.2.cloned.1.call-start
  6.5 3.3 %fusion.1 = f32[32768]{0:T(1024)} fusion(bf16[40,32768]{1,0:T(8,128)(2,1)} %param.5), kind=kLoop, calls=%fused_computation.6 | loop fusion | flops 3899392 | bytes 2752512 | tf_op jit(solution)/shard_map/reduce_sum | solution.py:63
  9.8 0.0 all-reduce.2.cloned.1.call-update
  9.8 0.8 dynamic_slice.3
  10.6 0.1 eq.28
  10.7 0.1 add.58
  10.8 0.1 fusion.20
  10.9 0.1 reduce_window_sum.11
  11.0 0.2 select_reduce_fusion
  11.3 0.1 sub.17
  11.3 0.8 compare_select_fusion
  12.1 0.0 copy-done.3
  12.1 46.1 %all-reduce.2.cloned.1.call-done = f32[32768]{0:T(1024)} async-done(((f32[32768]{0:T(1024)}), f32[32768]{0:T(1024)}) %all-reduce.2.cloned.1.call-update) | async-done | bytes 131088 | tf_op jit(solution)/shard_map/psum | solution.py:63
  58.2 0.9 add_rsqrt_fusion
  59.2 0.0 copy-done.1
  59.2 2.5 fusion.11
  61.7 0.1 broadcast_in_dim.4
  61.8 7.3 %scatter_fusion = bf16[512,2,128]{2,1,0:T(2,128)(2,1)S(1)} fusion(bf16[512,2,128]{2,1,0:T(2,128)(2,1)S(1)} %broadcast_in_dim.4, s32[256]{0:T(256)S(1)} %compare_select_fusion, bf16[256,2,128]{2,1,0:T(2,128)(2,1)S(1)} %fusion.11), kind=kCustom, calls=%fused_computation.1 | custom fusion | bytes 394240 | tf_op jit(solution)/shard_map/scatter | solution.py:85
  69.1 24.5 %all_to_all.25 = bf16[64,8,2,128]{3,1,2,0:T(8,128)(2,1)S(1)} all-to-all(bf16[64,8,2,128]{3,1,2,0:T(8,128)(2,1)S(1)} %copy.33), channel_id=1, replica_groups=mesh['wide'=64,'seq'=4] {'wide'}, dimensions={0} | all-to-all | bytes 524288 | tf_op jit(solution)/shard_map/all_to_all | solution.py:90
  93.7 0.0 copy-done
  93.7 3.2 %convolution_convert_fusion = bf16[64,8,2,2048]{3,1,2,0:T(8,128)(2,1)} fusion(bf16[64,8,2,128]{3,1,2,0:T(8,128)(2,1)S(1)} %all_to_all.25, bf16[1,128,2048]{2,1,0:T(8,128)(2,1)S(1)} %copy-done), kind=kOutput, calls=%fused_computation.10 | convolution fusion | flops 538968064 | bytes 4980736 | tf_op jit(solution)/shard_map/abtc,cd->abtd/dot_general | solution.py:38
  96.9 6.2 %all-to-all-start.1 = ((bf16[64,8,2,2048]{3,1,2,0:T(8,128)(2,1)}), bf16[64,8,2,2048]{3,1,2,0:T(8,128)(2,1)}, u32[]{:S(2)}, u32[]{:S(2)}) async-start(bf16[64,8,2,2048]{3,1,2,0:T(8,128)(2,1)} %convolution_convert_fusion), calls=%async_computation.1 | async-start | bytes 8388608 | tf_op jit(solution)/shard_map/all_to_all | solution.py:88
  103.1 95.8 %all-to-all-done.1 = bf16[64,8,2,2048]{3,1,2,0:T(8,128)(2,1)} async-done(((bf16[64,8,2,2048]{3,1,2,0:T(8,128)(2,1)}), bf16[64,8,2,2048]{3,1,2,0:T(8,128)(2,1)}, u32[]{:S(2)}, u32[]{:S(2)}) %all-to-all-start.1) | async-done | bytes 4194336 | tf_op jit(solution)/shard_map/all_to_all | solution.py:88
  198.9 2.5 copy.50
  201.4 6.2 %copy.35 = bf16[512,2,2048]{2,1,0:T(2,128)(2,1)} copy(bf16[512,2,2048]{2,0,1:T(8,128)(2,1)S(1)} %bitcast.54) | data formatting | bytes 8388608 | tf_op jit(solution)/shard_map/reshape | solution.py:97
  207.7 12.7 %gather_fusion = bf16[256,2,2048]{2,1,0:T(2,128)(2,1)S(1)} fusion(bf16[512,2,2048]{2,1,0:T(2,128)(2,1)} %copy.35, s32[1024]{0:T(1024)S(1)} %pad_clamp_fusion), kind=kCustom, calls=%fused_computation | custom fusion | bytes 4195328 | tf_op jit(solution)/shard_map/gather | solution.py:97
  220.4 28.8 %all_to_all.26 = bf16[256,2,2048]{2,1,0:T(2,128)(2,1)S(1)} all-to-all(bf16[256,2,2048]{2,1,0:T(2,128)(2,1)S(1)} %gather_fusion), channel_id=1, replica_groups=mesh['wide'=64,'seq'=4] {'seq'}, dimensions={0} | all-to-all | bytes 4194304 | tf_op jit(solution)/shard_map/all_to_all | solution.py:100
  249.3 2.5 copy.51
  251.8 2.2 reshape.56
  254.0 8.0 %fusion.24 = (f32[64,8,1536]{2,1,0:T(8,128)S(1)}, bf16[64,8,1536]{2,1,0:T(8,128)(2,1)}) fusion(bf16[512,2048]{1,0:T(8,128)(2,1)} %reshape.56, bf16[2048,1536]{1,0:T(8,128)(2,1)} %param.9), kind=kOutput, calls=%fused_computation.48 | convolution fusion | flops 3222798336 | bytes 13107200 | tf_op jit(solution)/shard_map/dot_general | solution.py:31
  262.0 0.0 copy-start.2
  262.0 1.7 copy-done.2
  263.7 0.3 multiply_reduce_fusion.1
  264.0 0.1 copy.37
  264.1 0.1 copy.38
  264.2 1.5 slice.16
  265.6 0.8 multiply_reduce_fusion
  266.5 0.1 copy.39
  266.6 0.2 copy.40
  266.8 7.2 %fusion.9 = f32[64,2,8,8,4]{3,2,4,1,0:T(8,128)} fusion(f32[64,8,2,4,128]{4,1,3,2,0:T(8,128)S(1)} %bitcast.56, f32[64,8,2,4]{1,3,2,0:T(4,128)S(1)} %copy.40, f32[64,8,1536]{2,1,0:T(8,128)} %copy-done.2, f32[64,8,2]{1,2,0:T(2,128)S(1)} %copy.38), kind=kOutput, calls=%fused_computation.17 | convolution fusion | flops 9043968 | bytes 2772992 | tf_op jit(solution)/shard_map/pigrd,pjgd->pgrij/dot_general | solution.py:23
  274.0 2.7 copy.41
  276.7 0.1 bitcast_reduce_fusion
  276.8 0.1 fusion.18
  276.9 1.6 copy.42
  278.4 2.3 convolution_convert_fusion.2
  (7 shorter events, 0.1 us)
Async XLA Ops:
  6.5 87.1 %copy-start = (bf16[1,128,2048]{2,1,0:T(8,128)(2,1)S(1)}, bf16[1,128,2048]{2,1,0:T(8,128)(2,1)}, u32[]{:S(2)}) copy-start(bf16[1,128,2048]{2,1,0:T(8,128)(2,1)} %param.8) | copy-start | bytes 1572868
  6.5 52.6 %copy-start.1 = (bf16[40,32768]{1,0:T(8,128)(2,1)S(1)}, bf16[40,32768]{1,0:T(8,128)(2,1)}, u32[]{:S(2)}) copy-start(bf16[40,32768]{1,0:T(8,128)(2,1)} %param.5) | copy-start | bytes 7864324
  6.5 5.6 %copy-start.3 = (s32[40]{0:T(128)S(1)}, s32[40]{0:T(128)}, u32[]{:S(2)}) copy-start(s32[40]{0:T(128)} %param.6) | copy-start | bytes 484
  6.5 51.7 %all-reduce.2.cloned.1.call-start = ((), (), s32[]{:S(2)}) async-start(), calls=%async_computation.3 | async-start | bytes 262144 | tf_op jit(solution)/shard_map/psum | solution.py:63
  96.9 102.1 %all-to-all-start.1 = ((bf16[64,8,2,2048]{3,1,2,0:T(8,128)(2,1)}), bf16[64,8,2,2048]{3,1,2,0:T(8,128)(2,1)}, u32[]{:S(2)}, u32[]{:S(2)}) async-start(bf16[64,8,2,2048]{3,1,2,0:T(8,128)(2,1)} %convolution_convert_fusion), calls=%async_computation.1 | async-start | bytes 8388608 | tf_op jit(solution)/shard_map/all_to_all | solution.py:88
  262.0 1.7 copy-start.2
Sparse Core Ops, SparseCore 0:
  10.0 48.2 all-reduce.1
where the time goes:
time: 288 us
  waiting for transfers between devices  142 us (49%)
  blocking collectives  53.4 us (19%)
  local copies, waits for them, and re-layouts  42.5 us (15%)
  matrix products  23.3 us (8%)
  between operations  13.6 us (5%)
  other arithmetic  6.75 us (2%)
  starting transfers between devices  6.24 us (2%)
    all_to_all x1, waiting for transfers between devices, body(): lax.all_to_all(readin_rows(lax.all_to_all(outgoing, 'wide', split_axis=0,...  95.8 us
    psum x1, waiting for transfers between devices, body(): squares = lax.psum(jnp.sum(signal * signal, axis=0), 'seq')  46.1 us
    all_to_all x1, blocking collectives, body(): lax.all_to_all(arrived, 'seq', split_axis=0, concat_axis=1, tiled=True)  28.8 us
    all_to_all x1, blocking collectives, body(): lax.all_to_all(outgoing, 'wide', split_axis=0, concat_axis=0, tiled=True)  24.5 us
    gather x1, local copies, waits for them, and re-layouts, body(): returned_rows.reshape(wide_count * slot_count, returned_rows.shape[2], re...  12.7 us
    dot_general x1, matrix products, project_rows(): jnp.dot(tokens.reshape(-1, tokens.shape[-1]), qkv_weight, preferred_eleme...  8.04 us
    scatter x1, local copies, waits for them, and re-layouts, body(): jnp.zeros((wide_count * slot_count, length, CH), jnp.bfloat16)  7.27 us
    dot_general x1, matrix products, attention_heads(): scores = jnp.einsum('pigrd,pjgd->pgrij', queries, key_rows) / HD ** 0.5  7.2 us
  transfers between devices with their start and end apart: 2, of which 2 were waited for; matrix products, arithmetic and copies ran while one was open for 1% of the time, Pallas kernels for 0%

commit v1 on v0

--- a/solution.py
+++ b/solution.py
@@ -60,7 +60,11 @@
     bin_count = sample_rows // SPB
     capacity = max(2, 2 * quarter // wide_count)
     signal = power.astype(jnp.float32)
-    squares = lax.psum(jnp.sum(signal * signal, axis=0), "seq")
+
+    def _bring_members_all(arr_in):
+        return jax.lax.all_gather(arr_in, "seq").sum(axis=0)
+
+    squares = _bring_members_all(jnp.sum(signal * signal, axis=0))
     inv_rms = 1.0 / jnp.sqrt(squares / (sample_rows * seq_count) + 1e-06)
     active = jnp.maximum(signal * inv_rms[None, :] - 0.8, 0.0)
     local_bins = bin_index - seq_index * bin_count

time: 288 us -> 246 us (0.85)
  waiting for transfers between devices: 142 us -> 95.8 us
  blocking collectives: 53.4 us -> 68.6 us
  between operations: 13.6 us -> 0.18 us
    psum x1 -> x0, waiting for transfers between devices: 46.1 us -> none  [body(): squares = lax.psum(jnp.sum(signal * signal, axis=0), 'seq')]
    all_gather x0 -> x1, blocking collectives: none -> 12.8 us  [_bring_members_all(): return jax.lax.all_gather(arr_in, 'seq').sum(axis=0)]
  transfers between devices with their start and end apart: 2 -> 1, of which waited for: 2 -> 1; matrix products, arithmetic and copies ran while one was open for 1% -> 0% of each run, Pallas kernels for 0% -> 0%
where the time goes in v1:
time: 246 us; the launch traced here: 245 us
  waiting for transfers between devices  95.8 us (39%)
  blocking collectives  68.6 us (28%)
  local copies, waits for them, and re-layouts  44.6 us (18%)
  matrix products  23.3 us (9%)
  other arithmetic  6.56 us (3%)
  starting transfers between devices  6.24 us (3%)
    all_to_all x1, waiting for transfers between devices, body(): lax.all_to_all(readin_rows(lax.all_to_all(outgoing, 'wide', split_axis=0,...  95.8 us
    all_to_all x1, blocking collectives, body(): lax.all_to_all(arrived, 'seq', split_axis=0, concat_axis=1, tiled=True)  29.8 us
    all_to_all x1, blocking collectives, body(): lax.all_to_all(outgoing, 'wide', split_axis=0, concat_axis=0, tiled=True)  26 us
    all_gather x1, blocking collectives, _bring_members_all(): return jax.lax.all_gather(arr_in, 'seq').sum(axis=0)  12.8 us
    gather x1, local copies, waits for them, and re-layouts, body(): returned_rows.reshape(wide_count * slot_count, returned_rows.shape[2], re...  12.7 us
    dot_general x1, matrix products, project_rows(): jnp.dot(tokens.reshape(-1, tokens.shape[-1]), qkv_weight, preferred_eleme...  8.04 us
    scatter x1, local copies, waits for them, and re-layouts, body(): jnp.zeros((wide_count * slot_count, length, CH), jnp.bfloat16)  7.27 us
    dot_general x1, matrix products, attention_heads(): scores = jnp.einsum('pigrd,pjgd->pgrij', queries, key_rows) / HD ** 0.5  7.2 us
  transfers between devices with their start and end apart: 1, of which 1 were waited for; matrix products, arithmetic and copies ran while one was open for 0% of the time, Pallas kernels for 0%

profile of v1, /device:TPU:1, one launch (start us, length us, event | category | flops | bytes accessed | tf_op | source)
XLA Modules:
  0.0 245.2 jit_solution(1706037250768357711)
XLA Ops:
  0.0 0.0 copy-start
  0.0 0.8 dynamic_slice.3
  0.8 0.1 eq.28
  0.9 0.1 add.60
  1.0 0.1 fusion.20
  1.1 0.1 reduce_window_sum.11
  1.2 0.2 select_reduce_fusion
  1.5 0.1 sub.17
  1.6 0.0 copy-start.3
  1.6 0.0 copy-start.1
  1.6 2.6 %fusion.1 = f32[32768]{0:T(1024)S(1)} fusion(bf16[40,32768]{1,0:T(8,128)(2,1)} %param.5), kind=kLoop, calls=%fused_computation.6 | loop fusion | flops 3899392 | bytes 2752512 | tf_op jit(solution)/shard_map/reduce_sum | solution.py:67
  4.2 12.8 %all-gather = f32[131072]{0:T(1024)} all-gather(f32[32768]{0:T(1024)S(1)} %fusion.1), channel_id=2, replica_groups=mesh['wide'=64,'seq'=4] {'seq'}, dimensions={0}, use_global_device_ids=true | all-gather | bytes 655360 | tf_op jit(solution)/shard_map/all_gather | solution.py:65
  17.0 2.1 reshape.81
  19.0 1.4 reduce_sum.56
  20.4 0.0 copy-done.3
  20.5 0.8 compare_select_fusion
  21.2 0.0 copy-done.1
  21.2 2.5 %fusion.11 = bf16[256,2,128]{2,1,0:T(2,128)(2,1)S(1)} fusion(bf16[40,32768]{1,0:T(8,128)(2,1)S(1)} %copy-done.1, f32[32768]{0:T(1024)S(1)} %add_rsqrt_fusion, s32[40]{0:T(128)S(1)} %broadcast_subtract_fusion), kind=kOutput, calls=%fused_computation.21 | convolution fusion | flops 36831312 | bytes 2883744 | tf_op jit(solution)/shard_map/dot_general | solution.py:74
  23.7 0.1 broadcast_in_dim.4
  23.9 7.3 %scatter_fusion = bf16[512,2,128]{2,1,0:T(2,128)(2,1)S(1)} fusion(bf16[512,2,128]{2,1,0:T(2,128)(2,1)S(1)} %broadcast_in_dim.4, s32[256]{0:T(256)S(1)} %compare_select_fusion, bf16[256,2,128]{2,1,0:T(2,128)(2,1)S(1)} %fusion.11), kind=kCustom, calls=%fused_computation.1 | custom fusion | bytes 394240 | tf_op jit(solution)/shard_map/scatter | solution.py:89
  31.2 26.0 %all_to_all.25 = bf16[64,8,2,128]{3,1,2,0:T(8,128)(2,1)S(1)} all-to-all(bf16[64,8,2,128]{3,1,2,0:T(8,128)(2,1)S(1)} %copy.47), channel_id=1, replica_groups=mesh['wide'=64,'seq'=4] {'wide'}, dimensions={0} | all-to-all | bytes 524288 | tf_op jit(solution)/shard_map/all_to_all | solution.py:94
  57.2 0.0 copy-done
  57.2 3.2 %convolution_convert_fusion = bf16[64,8,2,2048]{3,1,2,0:T(8,128)(2,1)} fusion(bf16[64,8,2,128]{3,1,2,0:T(8,128)(2,1)S(1)} %all_to_all.25, bf16[1,128,2048]{2,1,0:T(8,128)(2,1)S(1)} %copy-done), kind=kOutput, calls=%fused_computation.10 | convolution fusion | flops 538968064 | bytes 4980736 | tf_op jit(solution)/shard_map/abtc,cd->abtd/dot_general | solution.py:38
  60.4 6.2 %all-to-all-start.1 = ((bf16[64,8,2,2048]{3,1,2,0:T(8,128)(2,1)}), bf16[64,8,2,2048]{3,1,2,0:T(8,128)(2,1)}, u32[]{:S(2)}, u32[]{:S(2)}) async-start(bf16[64,8,2,2048]{3,1,2,0:T(8,128)(2,1)} %convolution_convert_fusion), calls=%async_computation.1 | async-start | bytes 8388608 | tf_op jit(solution)/shard_map/all_to_all | solution.py:92
  66.7 95.8 %all-to-all-done.1 = bf16[64,8,2,2048]{3,1,2,0:T(8,128)(2,1)} async-done(((bf16[64,8,2,2048]{3,1,2,0:T(8,128)(2,1)}), bf16[64,8,2,2048]{3,1,2,0:T(8,128)(2,1)}, u32[]{:S(2)}, u32[]{:S(2)}) %all-to-all-start.1) | async-done | bytes 4194336 | tf_op jit(solution)/shard_map/all_to_all | solution.py:92
  162.5 2.5 %copy.64 = bf16[64,8,2,2048]{3,1,0,2:T(8,128)(2,1)S(1)} copy(bf16[64,8,2,2048]{3,1,2,0:T(8,128)(2,1)} %all-to-all-done.1) | data formatting | bytes 8388608 | tf_op jit(solution)/shard_map/all_to_all | solution.py:92
  165.0 6.2 %copy.49 = bf16[512,2,2048]{2,1,0:T(2,128)(2,1)} copy(bf16[512,2,2048]{2,0,1:T(8,128)(2,1)S(1)} %bitcast.54) | data formatting | bytes 8388608 | tf_op jit(solution)/shard_map/reshape | solution.py:101
  171.2 12.7 %gather_fusion = bf16[256,2,2048]{2,1,0:T(2,128)(2,1)S(1)} fusion(bf16[512,2,2048]{2,1,0:T(2,128)(2,1)} %copy.49, s32[1024]{0:T(1024)S(1)} %pad_clamp_fusion), kind=kCustom, calls=%fused_computation | custom fusion | bytes 4195328 | tf_op jit(solution)/shard_map/gather | solution.py:101
  184.0 29.8 %all_to_all.26 = bf16[256,2,2048]{2,1,0:T(2,128)(2,1)S(1)} all-to-all(bf16[256,2,2048]{2,1,0:T(2,128)(2,1)S(1)} %gather_fusion), channel_id=1, replica_groups=mesh['wide'=64,'seq'=4] {'seq'}, dimensions={0} | all-to-all | bytes 4194304 | tf_op jit(solution)/shard_map/all_to_all | solution.py:104
  213.8 2.5 %copy.65 = bf16[4,64,2,2048]{3,2,0,1:T(2,128)(2,1)S(1)} copy(bf16[4,64,2,2048]{3,2,1,0:T(2,128)(2,1)S(1)} %bitcast.57) | data formatting | bytes 4194304 | tf_op jit(solution)/shard_map/all_to_all | solution.py:104
  216.2 2.2 reshape.60
  218.5 8.0 %fusion.24 = (f32[64,8,1536]{2,1,0:T(8,128)S(1)}, bf16[64,8,1536]{2,1,0:T(8,128)(2,1)}) fusion(bf16[512,2048]{1,0:T(8,128)(2,1)} %reshape.60, bf16[2048,1536]{1,0:T(8,128)(2,1)} %param.9), kind=kOutput, calls=%fused_computation.48 | convolution fusion | flops 3222798336 | bytes 13107200 | tf_op jit(solution)/shard_map/dot_general | solution.py:31
  226.5 0.0 copy-start.2
  226.5 1.7 copy-done.2
  228.2 0.3 multiply_reduce_fusion.1
  228.4 0.1 copy.51
  228.5 0.1 copy.52
  228.6 1.5 slice.16
  230.1 0.8 multiply_reduce_fusion
  230.9 0.1 copy.53
  231.1 0.2 copy.54
  231.3 7.2 %fusion.9 = f32[64,2,8,8,4]{3,2,4,1,0:T(8,128)} fusion(f32[64,8,2,4,128]{4,1,3,2,0:T(8,128)S(1)} %bitcast.56, f32[64,8,2,4]{1,3,2,0:T(4,128)S(1)} %copy.54, f32[64,8,1536]{2,1,0:T(8,128)} %copy-done.2, f32[64,8,2]{1,2,0:T(2,128)S(1)} %copy.52), kind=kOutput, calls=%fused_computation.17 | convolution fusion | flops 9043968 | bytes 2772992 | tf_op jit(solution)/shard_map/pigrd,pjgd->pgrij/dot_general | solution.py:23
  238.5 2.7 %copy.55 = f32[64,2,8,8,4]{0,2,3,4,1:T(8,128)S(1)} copy(f32[64,2,8,8,4]{3,2,4,1,0:T(8,128)} %fusion.9) | data formatting | bytes 262144 | tf_op jit(solution)/shard_map/pigrd,pjgd->pgrij/dot_general | solution.py:23
  241.1 0.1 bitcast_reduce_fusion
  241.2 0.1 fusion.18
  241.3 1.6 copy.56
  242.9 2.3 convolution_convert_fusion.2
  (8 shorter events, 0.1 us)
Async XLA Ops:
  0.0 57.2 %copy-start = (bf16[1,128,2048]{2,1,0:T(8,128)(2,1)S(1)}, bf16[1,128,2048]{2,1,0:T(8,128)(2,1)}, u32[]{:S(2)}) copy-start(bf16[1,128,2048]{2,1,0:T(8,128)(2,1)} %param.8) | copy-start | bytes 1572868
  1.6 18.9 %copy-start.3 = (s32[40]{0:T(128)S(1)}, s32[40]{0:T(128)}, u32[]{:S(2)}) copy-start(s32[40]{0:T(128)} %param.6) | copy-start | bytes 484
  1.6 19.7 %copy-start.1 = (bf16[40,32768]{1,0:T(8,128)(2,1)S(1)}, bf16[40,32768]{1,0:T(8,128)(2,1)}, u32[]{:S(2)}) copy-start(bf16[40,32768]{1,0:T(8,128)(2,1)} %param.5) | copy-start | bytes 7864324
  60.4 102.1 %all-to-all-start.1 = ((bf16[64,8,2,2048]{3,1,2,0:T(8,128)(2,1)}), bf16[64,8,2,2048]{3,1,2,0:T(8,128)(2,1)}, u32[]{:S(2)}, u32[]{:S(2)}) async-start(bf16[64,8,2,2048]{3,1,2,0:T(8,128)(2,1)} %convolution_convert_fusion), calls=%async_computation.1 | async-start | bytes 8388608 | tf_op jit(solution)/shard_map/all_to_all | solution.py:92
  226.5 1.7 copy-start.2
